TPU v7x, 32 devices: a whole 2x2x4 slice. The times are simulated.
32 devices in a mesh: group: 4 (over z), member: 8 (over y, x, core).
Axes of the slice: x: 2, y: 2, z: 4, core: 2. Of those that a mesh axis runs over, the one named last changes fastest.
Arguments:
- query_feat: bfloat16 [4096, 4096], P(('group', 'member'))
- code_feat: bfloat16 [4096, 4096], P(('group', 'member'))
- projection: bfloat16 [4096, 1024], replicated
- hard_ids: int32 [32, 16], P(('group', 'member')), may hold values from 0 to 63, as said below
- loss_weight: float32 [4096], P(('group', 'member')), may hold values from 1 to 4
Outputs:
- query_grad: bfloat16 [4096, 4096], P(('group', 'member'))
- code_grad: bfloat16 [4096, 4096], P(('group', 'member'))
- projection_grad: float32 [4096, 1024], P(('group', 'member'))
Inputs may be any that keep to these rules, and one draw needn't show every extreme that they name: `hard_ids`: entry (owner device g * 8 + m) * 2 + slot names code rows of that device. A row names 16 different blocks, none of its own group; at most 8 of them lie in one group, and exactly 8 in some group of every row.
All inputs are finite; a program needn't handle non-finite values.
Results may differ from a plain program's by a relative error of at most 0.02.
Values may be sent and summed in bfloat16 or wider, within the bound.
No kernel may reach another device: no remote copies, remote signals or barrier semaphores. Data moves between devices by JAX's collectives and lax.ppermute only.
A program may use at most 128 MiB of HBM per device.

v0:
```python
import jax
import jax.numpy as jnp
from jax import lax
from jax.sharding import PartitionSpec as P

CB = 64
inverse_temp = 120.0
epsilon = 1e-06


def embed(features, projection):
    values = jnp.dot(features, projection, preferred_element_type=jnp.float32)
    inverse = lax.rsqrt(jnp.sum(values * values, axis=1) + epsilon)
    unit_vec = values * inverse[:, None]
    return (unit_vec, inverse, unit_vec.astype(jnp.bfloat16))


def norm_back(upstream, unit_vec, inverse):
    inner_prod = jnp.sum(unit_vec * upstream, axis=1, keepdims=True)
    return (inverse[:, None] * (upstream - unit_vec * inner_prod)).astype(jnp.bfloat16)


def shift_all(x, axis):
    size = lax.axis_size(axis)
    index = lax.axis_index(axis)
    got = [x]
    for s in range(1, size):
        got.append(lax.ppermute(x, axis, [(i, (i + s) % size) for i in range(size)]))
    order = (index - jnp.arange(size)) % size
    return jax.tree.map(lambda *xs: jnp.take(jnp.stack(xs, axis=0), order, axis=0), *got)


def exchange(parts, axis):
    size = lax.axis_size(axis)
    index = lax.axis_index(axis)
    got = [jnp.take(parts, index, axis=0)]
    for s in range(1, size):
        sent = jnp.take(parts, (index + s) % size, axis=0)
        got.append(lax.ppermute(sent, axis, [(i, (i + s) % size) for i in range(size)]))
    stacked = jnp.stack(got, axis=0)
    return jnp.take(stacked, (index - jnp.arange(size)) % size, axis=0)


def body(query_feat, code_feat, projection, hard_ids, loss_weight):
    groups = lax.axis_size("group")
    members = lax.axis_size("member")
    group_index = lax.axis_index("group")
    member_index = lax.axis_index("member")
    queries_dev = query_feat.shape[0]
    feat_width = query_feat.shape[1]
    emb_width = projection.shape[1]
    slot_count = queries_dev // CB
    per_group = members * slot_count
    group_span = members * queries_dev
    rows_dev = feat_width // (groups * members)
    feats = jnp.stack([query_feat, code_feat], axis=0).reshape(
        2, queries_dev, groups, members, rows_dev
    )
    feats = jnp.transpose(feats, (3, 0, 1, 2, 4))
    feat_cols = lax.all_to_all(feats, "member", split_axis=0, concat_axis=0, tiled=True)
    q_unit, q_inv, q_emb = embed(query_feat, projection)
    code_values = lax.all_gather(
        jnp.dot(code_feat, projection, preferred_element_type=jnp.float32),
        "member",
        axis=0,
        tiled=True,
    )
    c_inv = lax.rsqrt(jnp.sum(code_values * code_values, axis=1) + epsilon)
    c_unit = code_values * c_inv[:, None]
    group_codes = c_unit.astype(jnp.bfloat16)
    q_all = lax.all_to_all(
        jnp.broadcast_to(q_emb[None], (groups, queries_dev, emb_width)),
        "group",
        split_axis=0,
        concat_axis=0,
        tiled=True,
    )
    ids_all = shift_all(hard_ids[0], "group")
    block_ids = group_index * per_group + jnp.arange(per_group, dtype=jnp.int32)
    asked = jnp.any(ids_all[:, :, None] == block_ids[None, None, :], axis=1)
    own = jnp.arange(groups, dtype=jnp.int32) == group_index
    block_mask = asked | own[:, None]
    col_mask = jnp.broadcast_to(block_mask[:, :, None], (groups, per_group, CB)).reshape(
        groups, 1, group_span
    )
    scores = inverse_temp * jnp.einsum(
        "gqe,ke->gqk", q_all, group_codes, preferred_element_type=jnp.float32
    )
    scores = jnp.where(col_mask, scores, -jnp.inf)
    part_max = jnp.max(scores, axis=2)
    safe_max = jnp.where(part_max > -jnp.inf, part_max, 0.0)
    part_sum = jnp.sum(jnp.exp(scores - safe_max[:, :, None]), axis=2)
    weights_row = jnp.broadcast_to(loss_weight[None], (groups, queries_dev))
    stats = shift_all(jnp.stack([part_max, part_sum, weights_row], axis=0), "group")
    w_all = stats[:, 2, 0]
    row_max = jnp.max(stats[:, 0], axis=0)
    row_sum = jnp.sum(stats[:, 1] * jnp.exp(stats[:, 0] - row_max[None]), axis=0)
    log_total = row_max + jnp.log(row_sum)
    offsets = jnp.arange(queries_dev, dtype=jnp.int32)
    columns = jnp.arange(group_span, dtype=jnp.int32)
    positive = (columns[None, :] == (member_index * queries_dev + offsets)[:, None]).astype(
        jnp.float32
    )
    positive = positive[None] * own[:, None, None].astype(jnp.float32)
    factor = w_all * inverse_temp
    grad = (factor[:, :, None] * (jnp.exp(scores - log_total[:, :, None]) - positive)).astype(
        jnp.bfloat16
    )
    code_terms = None
    for g in range(groups):
        term = jnp.dot(grad[g].T, q_all[g], preferred_element_type=jnp.float32)
        term = jnp.where(g == group_index, term, term.astype(jnp.bfloat16).astype(jnp.float32))
        code_terms = term if code_terms is None else code_terms + term
    code_sum = code_terms.astype(jnp.bfloat16)
    grad_dq, code_sum = lax.optimization_barrier((grad, code_sum))
    code_delta = lax.psum(code_sum, "member").astype(jnp.float32)
    delta_parts = jnp.einsum(
        "gqk,ke->gqe", grad_dq, group_codes, preferred_element_type=jnp.float32
    )
    returned = exchange(delta_parts.astype(jnp.bfloat16), "group").astype(jnp.float32)
    own_part = jnp.take(delta_parts, group_index, axis=0)
    query_delta = own_part + jnp.sum(jnp.where(own[:, None, None], 0.0, returned), axis=0)
    dz_query = norm_back(query_delta, q_unit, q_inv)
    dz_code_all = norm_back(code_delta, c_unit, c_inv)
    dz_code = lax.dynamic_slice_in_dim(dz_code_all, member_index * queries_dev, queries_dev, 0)
    query_grad = jnp.einsum(
        "qe,de->qd", dz_query, projection, preferred_element_type=jnp.float32
    ).astype(jnp.bfloat16)
    code_grad = jnp.einsum(
        "qe,de->qd", dz_code, projection, preferred_element_type=jnp.float32
    ).astype(jnp.bfloat16)
    dzq_all = lax.all_to_all(
        jnp.broadcast_to(dz_query[None], (members, queries_dev, emb_width)),
        "member",
        split_axis=0,
        concat_axis=0,
        tiled=True,
    )
    dzc_all = dz_code_all.reshape(members, queries_dev, emb_width)
    proj_parts = jnp.einsum(
        "mqgr,mqe->gre", feat_cols[:, 0], dzq_all, preferred_element_type=jnp.float32
    ) + jnp.einsum("mqgr,mqe->gre", feat_cols[:, 1], dzc_all, preferred_element_type=jnp.float32)
    own_proj = jnp.take(proj_parts, group_index, axis=0)
    sent_proj = jnp.where(own[:, None, None], 0.0, proj_parts).astype(jnp.bfloat16)
    projection_grad = own_proj + lax.psum_scatter(
        sent_proj, "group", scatter_dimension=0, tiled=True
    ).reshape(rows_dev, emb_width).astype(jnp.float32)
    return (query_grad, code_grad, projection_grad)


def solution(mesh):
    return jax.shard_map(
        body,
        mesh=mesh,
        in_specs=(
            P(("group", "member"), None),
            P(("group", "member"), None),
            P(),
            P(("group", "member"), None),
            P(("group", "member")),
        ),
        out_specs=(
            P(("group", "member"), None),
            P(("group", "member"), None),
            P(("group", "member"), None),
        ),
        check_vma=False,
    )
```

profile of v0, /device:TPU:0, one launch (start us, length us, event | category | flops | bytes accessed | tf_op | source)
XLA Modules:
  0.0 204.6 jit_solution(2245639925189366476)
XLA Ops:
  7.2 5.8 %fusion.26 = f32[128,1024]{1,0:T(8,128)} fusion(bf16[128,4096]{1,0:T(8,128)(2,1)} %param.10, bf16[4096,1024]{1,0:T(8,128)(2,1)} %param.11), kind=kOutput, calls=%fused_computation.91 | convolution fusion | flops 1073741824 | bytes 9961472 | tf_op jit(solution)/shard_map/dot_general | solution.py:63
  13.1 3.1 %collective-permute-start = (s32[16]{0:T(128)S(1)}, s32[16]{0:T(128)S(1)}, u32[]{:S(2)}, u32[]{:S(2)}) collective-permute-start(s32[16]{0:T(128)S(1)} %bitcast.128), channel_id=1, source_target_pairs={{0,8},{8,16},{16,24},{24,0},{1,9},{9,17},{17,25},{25,1},{2,10},{10... | collective-permute-start | bytes 200 | tf_op jit(solution)/shard_map/ppermute | solution.py:28
  16.2 2.6 %collective-permute-start.1 = (s32[16]{0:T(128)S(1)}, s32[16]{0:T(128)S(1)}, u32[]{:S(2)}, u32[]{:S(2)}) collective-permute-start(s32[16]{0:T(128)S(1)} %bitcast.129), channel_id=1, source_target_pairs={{0,16},{8,24},{16,0},{24,8},{1,17},{9,25},{17,1},{25,9},{2,18},{10... | collective-permute-start | bytes 200 | tf_op jit(solution)/shard_map/ppermute | solution.py:28
  18.8 1.4 collective-permute-start.2
  20.2 5.0 %multiply_reduce_fusion.2 = (f32[128]{0:T(128)S(1)}, f32[128,1024]{1,0:T(8,128)S(1)}) fusion(bf16[128,4096]{1,0:T(8,128)(2,1)S(1)} %copy-done.5, bf16[4096,1024]{1,0:T(8,128)(2,1)} %param.11), kind=kOutput, calls=%fused_computation.31 | convolution fusion | flops 1074003840 | bytes 9961984 | tf_op jit(solution)/shard_map/dot_general | solution.py:12
  25.2 0.1 multiply_convert_fusion.3
  25.3 1.1 broadcast_in_dim.126
  26.4 3.6 %all-to-all-start = ((bf16[4,128,1024]{2,1,0:T(8,128)(2,1)}), bf16[4,128,1024]{2,1,0:T(8,128)(2,1)S(1)}, u32[]{:S(2)}, u32[]{:S(2)}) async-start(bf16[4,128,1024]{2,1,0:T(8,128)(2,1)} %broadcast_in_dim.126), calls=%async_computation | async-start | bytes 2097152 | tf_op jit(solution)/shard_map/all_to_all | solution.py:71
  30.1 1.3 copy.23
  31.4 1.3 copy.24
  32.8 1.4 maximum_bitcast_fusion
  34.2 0.9 fusion.6
  35.1 1.5 copy.25
  36.6 0.6 gather_fusion
  37.1 0.1 broadcast_select_fusion.1
  37.2 0.1 compare_reduce_fusion
  37.3 0.1 broadcast_or_fusion
  37.4 0.1 broadcast_in_dim.123
  37.4 0.1 broadcast_in_dim.124
  37.5 15.0 %all-gather.2.cloned.1.call-done = f32[1024,1024]{1,0:T(8,128)} async-done(((f32[128,1024]{1,0:T(8,128)}), f32[1024,1024]{1,0:T(8,128)}) %all-gather.2.cloned.1.call-update) | async-done | bytes 4194320 | tf_op jit(solution)/shard_map/all_gather | solution.py:62
  52.6 2.5 %multiply_reduce_fusion = f32[1024]{0:T(1024)S(1)} fusion(f32[1024,1024]{1,0:T(8,128)} %all-gather.2.cloned.1.call-done), kind=kLoop, calls=%fused_computation.11 | loop fusion | flops 2096128 | bytes 4198400 | tf_op jit(solution)/shard_map/reduce_sum | solution.py:68
  55.1 4.4 %all-to-all-start.1 = ((bf16[8,2,128,4,128]{2,4,3,1,0:T(8,128)(2,1)}), bf16[8,2,128,4,128]{2,4,3,1,0:T(8,128)(2,1)}, u32[]{:S(2)}, u32[]{:S(2)}) async-start(bf16[8,2,128,4,128]{2,4,3,1,0:T(8,128)(2,1)} %copy.25), calls=%async_computation.1 | async-start | bytes 4194304 | tf_op jit(solution)/shard_map/all_to_all | solution.py:60
  59.5 3.6 %fusion.24 = (f32[4,128]{1,0:T(4,128)S(1)}, f32[4,128,1024]{2,1,0:T(8,128)S(1)}) fusion(bf16[4,128,1024]{2,1,0:T(8,128)(2,1)S(1)} %all-to-all-done, f32[1024,1024]{1,0:T(8,128)} %all-gather.2.cloned.1.call-done, f32[1024]{0:T(1024)S(1)} %add_rsqrt_fusion, pred[4,1024]{1,0:T(4,128)(4,1)S(1)} %broadcast_in_dim.124), kind=kOutput, calls=%fused_computation.89 | convolution fusion | flops 1077411328 | bytes 7350272 | tf_op jit(solution)/shard_map/gqe,ke->gqk/dot_general | solution.py:86
  63.2 0.5 exponential_reduce_fusion
  63.7 0.2 copy-done.8
  63.8 2.5 %collective-permute-start.4 = (f32[3,4,128]{2,1,0:T(4,128)S(1)}, f32[3,4,128]{2,1,0:T(4,128)S(1)}, u32[]{:S(2)}, u32[]{:S(2)}) collective-permute-start(f32[3,4,128]{2,1,0:T(4,128)S(1)} %get-tuple-element.38), channel_id=1, source_target_pairs={{0,16},{8,24},{16,0},{24,8},{1,17},{9,25},{17,1},{25,9},{2,18},{10... | collective-permute-start | bytes 18440 | tf_op jit(solution)/shard_map/ppermute | solution.py:28
  66.3 1.4 collective-permute-start.5
  67.7 0.6 collective-permute-start.3
  68.3 0.1 collective-permute-done.4
  68.4 1.5 collective-permute-done.5
  69.9 3.2 %collective-permute-done.3 = f32[3,4,128]{2,1,0:T(4,128)S(1)} collective-permute-done((f32[3,4,128]{2,1,0:T(4,128)S(1)}, f32[3,4,128]{2,1,0:T(4,128)S(1)}, u32[]{:S(2)}, u32[]{:S(2)}) %collective-permute-start.3) | collective-permute-done | bytes 6176 | tf_op jit(solution)/shard_map/ppermute | solution.py:28
  73.2 0.6 gather_fusion.1
  73.8 0.1 broadcast_select_fusion
  73.9 1.6 multiply_convert_fusion.1
  75.5 0.7 fusion.11
  76.2 0.7 fusion.12
  76.9 0.7 fusion.10
  77.7 2.4 %add_convert_fusion = bf16[1024,1024]{1,0:T(8,128)(2,1)} fusion(f32[1024,1024]{1,0:T(8,128)S(1)} %fusion.10, f32[1024,1024]{1,0:T(8,128)S(1)} %fusion.11, f32[1024,1024]{1,0:T(8,128)S(1)} %fusion.12, pred[]{:T(512)S(6)} %eq.75, pred[]{:T(512)S(6)} %eq.74, pred[]{:T(512)S(6)} %eq.73, pred[]{:T(512)S(6)} %eq.72, bf16[4,128,1024]{2,1,0:T(8,128)(2,1)S(1)} %all-to-all-done, ...), kind=kOutput, calls=%fused_computation.10 | convolution fusion | flops 285212672 | bytes 15204356 | tf_op jit(solution)/shard_map/dot_general | solution.py:111
  80.1 3.8 %fusion.25 = (bf16[4,128,1024]{2,1,0:T(8,128)(2,1)S(1)}, f32[4,128,1024]{2,1,0:T(8,128)S(1)}) fusion(bf16[4,128,1024]{2,1,0:T(8,128)(2,1)} %copy-done.1, f32[1024,1024]{1,0:T(8,128)} %all-gather.2.cloned.1.call-done, f32[1024]{0:T(1024)S(1)} %add_rsqrt_fusion), kind=kOutput, calls=%fused_computation.90 | convolution fusion | flops 1076363264 | bytes 8392704 | tf_op jit(solution)/shard_map/gqk,ke->gqe/dot_general | solution.py:117
  83.9 0.9 dynamic-slice_select_fusion
  84.9 0.6 collective-permute-start.7
  85.4 3.3 %collective-permute-start.8 = (bf16[128,1024]{1,0:T(8,128)(2,1)}, bf16[128,1024]{1,0:T(8,128)(2,1)S(1)}, u32[]{:S(2)}, u32[]{:S(2)}) collective-permute-start(bf16[128,1024]{1,0:T(8,128)(2,1)} %get-tuple-element.34), channel_id=1, source_target_pairs={{0,24},{8,0},{16,8},{24,16},{1,25},{9,1},{17,9},{25,17},{2,26},{10... | collective-permute-start | bytes 786440 | tf_op jit(solution)/shard_map/ppermute | solution.py:39
  88.7 7.4 %collective-permute-done.6 = bf16[128,1024]{1,0:T(8,128)(2,1)S(1)} collective-permute-done((bf16[128,1024]{1,0:T(8,128)(2,1)}, bf16[128,1024]{1,0:T(8,128)(2,1)S(1)}, u32[]{:S(2)}, u32[]{:S(2)}) %collective-permute-start.6) | collective-permute-done | bytes 262176 | tf_op jit(solution)/shard_map/ppermute | solution.py:39
  96.2 8.9 %collective-permute-done.7 = bf16[128,1024]{1,0:T(8,128)(2,1)S(1)} collective-permute-done((bf16[128,1024]{1,0:T(8,128)(2,1)}, bf16[128,1024]{1,0:T(8,128)(2,1)S(1)}, u32[]{:S(2)}, u32[]{:S(2)}) %collective-permute-start.7) | collective-permute-done | bytes 262176 | tf_op jit(solution)/shard_map/ppermute | solution.py:39
  105.1 1.1 pad_maximum_fusion
  106.2 2.9 %gather_fusion.2 = bf16[4,128,1024]{2,1,0:T(8,128)(2,1)} fusion(bf16[4,128,1024]{2,1,0:T(8,128)(2,1)} %pad_maximum_fusion, s32[1024]{0:T(1024)S(1)} %pad_clamp_fusion), kind=kCustom, calls=%fused_computation.2 | custom fusion | bytes 2097168 | tf_op jit(solution)/shard_map/jit(_take)/gather | solution.py:41
  109.1 1.6 select_reduce_fusion
  110.7 0.2 multiply_reduce_fusion.1
  110.9 0.2 multiply_convert_fusion.2
  111.1 1.6 broadcast_in_dim.134
  112.7 4.3 %all-to-all-start.2 = ((bf16[8,128,1024]{2,1,0:T(8,128)(2,1)}), bf16[8,128,1024]{2,1,0:T(8,128)(2,1)}, u32[]{:S(2)}, u32[]{:S(2)}) async-start(bf16[8,128,1024]{2,1,0:T(8,128)(2,1)} %broadcast_in_dim.134), calls=%async_computation.2 | async-start | bytes 4194304 | tf_op jit(solution)/shard_map/all_to_all | solution.py:132
  117.1 0.0 reduce-scatter.2.cloned.1.call-start
  117.1 2.8 %fusion.23 = (bf16[8,1,128,4,128]{2,4,3,1,0:T(8,128)(2,1)S(1)}, bf16[8,1,128,4,128]{2,4,3,1,0:T(8,128)(2,1)}) fusion(bf16[8,2,128,4,128]{2,4,3,1,0:T(8,128)(2,1)} %all-to-all-done.1), kind=kLoop, calls=%fused_computation.88 | loop fusion | bytes 4194304 | tf_op jit(solution)/shard_map/slice | solution.py:142
  119.9 37.8 %all-reduce.2.cloned.1.call-done = bf16[1024,1024]{1,0:T(8,128)(2,1)} async-done(((bf16[1024,1024]{1,0:T(8,128)(2,1)}), bf16[1024,1024]{1,0:T(8,128)(2,1)}) %all-reduce.2.cloned.1.call-update) | async-done | bytes 2097168 | tf_op jit(solution)/shard_map/psum | solution.py:116
  157.7 3.7 %fusion = f32[1024]{0:T(1024)S(1)} fusion(bf16[1024,1024]{1,0:T(8,128)(2,1)} %all-reduce.2.cloned.1.call-done, f32[1024,1024]{1,0:T(8,128)} %all-gather.2.cloned.1.call-done, f32[1024]{0:T(1024)S(1)} %add_rsqrt_fusion), kind=kLoop, calls=%fused_computation.7 | loop fusion | flops 4193280 | bytes 6299648 | tf_op jit(solution)/shard_map/reduce_sum | solution.py:19
  161.3 0.4 copy-done
  161.7 0.7 copy-done.2
  162.4 0.8 fusion.2
  163.2 3.2 %fusion.4 = f32[4,128,1024,1]{2,1,3,0:T(8,128)S(1)} fusion(bf16[8,128,1024]{2,1,0:T(8,128)(2,1)} %all-to-all-done.2, bf16[8,1,128,4,128]{2,4,3,1,0:T(8,128)(2,1)} %get-tuple-element.32), kind=kOutput, calls=%fused_computation.16 | convolution fusion | flops 1073741824 | bytes 5242880 | tf_op jit(solution)/shard_map/mqgr,mqe->gre/dot_general | solution.py:140
  166.4 2.9 %select_convert_fusion = (bf16[4,128,1024]{2,1,0:T(8,128)(2,1)}, f32[4,128,1024]{2,1,0:T(8,128)}) fusion(pred[4]{0:T(512)(128)(4,1)S(1)} %iota_compare_fusion.1, bf16[8,128,1024,1]{2,1,0,3:T(8,128)(2,1)S(1)} %bitcast.116, bf16[8,1,128,4,128]{2,4,3,1,0:T(8,128)(2,1)S(1)} %get-tuple-element.31, f32[4,128,1024,1]{2,1,3,0:T(8,128)S(1)} %fusion.4), kind=kOutput, calls=%fused_computation.18 | convolution fusion | flops 1074790400 | bytes 8388612 | tf_op jit(solution)/shard_map/mqgr,mqe->gre/dot_general | solution.py:142
  169.3 7.2 %convolution_convert_fusion.1 = bf16[128,4096]{1,0:T(8,128)(2,1)} fusion(bf16[128,1024]{1,0:T(8,128)(2,1)S(1)} %multiply_convert_fusion.2, bf16[4096,1024]{1,0:T(8,128)(2,1)} %param.11), kind=kOutput, calls=%fused_computation.6 | convolution fusion | flops 1074266112 | bytes 9699328 | tf_op jit(solution)/shard_map/qe,de->qd/dot_general | solution.py:126
  176.6 7.2 %convolution_convert_fusion = bf16[128,4096]{1,0:T(8,128)(2,1)} fusion(bf16[4096,1024]{1,0:T(8,128)(2,1)} %param.11, bf16[1024,1024]{1,0:T(8,128)(2,1)S(1)} %fusion.2, s32[]{:T(128)S(6)} %select_n.153), kind=kOutput, calls=%fused_computation.5 | convolution fusion | flops 1074266112 | bytes 9699332 | tf_op jit(solution)/shard_map/qe,de->qd/dot_general | solution.py:129
  183.8 12.3 %reduce-scatter.2.cloned.1.call-done = bf16[1,128,1024]{2,1,0:T(8,128)(2,1)} async-done(((bf16[4,128,1024]{2,1,0:T(8,128)(2,1)}), bf16[1,128,1024]{2,1,0:T(8,128)(2,1)}) %reduce-scatter.2.cloned.1.call-update) | async-done | bytes 262160 | tf_op jit(solution)/shard_map/reduce_scatter | solution.py:145
  196.1 2.0 convert_add_fusion
  (48 shorter events, 0.3 us)
Async XLA Ops:
  7.2 5.9 %copy-start.9 = (s32[1,16]{1,0:T(1,128)S(1)}, s32[1,16]{1,0:T(1,128)}, u32[]{:S(2)}) copy-start(s32[1,16]{1,0:T(1,128)} %param.12) | copy-start | bytes 196
  7.2 13.0 %copy-start.5 = (bf16[128,4096]{1,0:T(8,128)(2,1)S(1)}, bf16[128,4096]{1,0:T(8,128)(2,1)}, u32[]{:S(2)}) copy-start(bf16[128,4096]{1,0:T(8,128)(2,1)} %param.9) | copy-start | bytes 3145732
  7.2 45.4 %all-gather.2.cloned.1.call-start = ((), (), s32[]{:S(2)}) async-start(), calls=%async_computation.4 | async-start | bytes 4718592 | tf_op jit(solution)/shard_map/all_gather | solution.py:62
  13.1 23.4 %collective-permute-start = (s32[16]{0:T(128)S(1)}, s32[16]{0:T(128)S(1)}, u32[]{:S(2)}, u32[]{:S(2)}) collective-permute-start(s32[16]{0:T(128)S(1)} %bitcast.128), channel_id=1, source_target_pairs={{0,8},{8,16},{16,24},{24,0},{1,9},{9,17},{17,25},{25,1},{2,10},{10... | collective-permute-start | bytes 200 | tf_op jit(solution)/shard_map/ppermute | solution.py:28
  16.2 20.3 %collective-permute-start.1 = (s32[16]{0:T(128)S(1)}, s32[16]{0:T(128)S(1)}, u32[]{:S(2)}, u32[]{:S(2)}) collective-permute-start(s32[16]{0:T(128)S(1)} %bitcast.129), channel_id=1, source_target_pairs={{0,16},{8,24},{16,0},{24,8},{1,17},{9,25},{17,1},{25,9},{2,18},{10... | collective-permute-start | bytes 200 | tf_op jit(solution)/shard_map/ppermute | solution.py:28
  18.8 17.7 %collective-permute-start.2 = (s32[16]{0:T(128)S(1)}, s32[16]{0:T(128)S(1)}, u32[]{:S(2)}, u32[]{:S(2)}) collective-permute-start(s32[16]{0:T(128)S(1)} %bitcast.130), channel_id=1, source_target_pairs={{0,24},{8,0},{16,8},{24,16},{1,25},{9,1},{17,9},{25,17},{2,26},{10... | collective-permute-start | bytes 200 | tf_op jit(solution)/shard_map/ppermute | solution.py:28
  25.1 1.2 copy-start.3
  26.4 5.1 %copy-start.6 = (bf16[128,4096]{1,0:T(8,128)(2,1)S(1)}, bf16[128,4096]{1,0:T(8,128)(2,1)}, u32[]{:S(2)}) copy-start(bf16[128,4096]{1,0:T(8,128)(2,1)} %param.10) | copy-start | bytes 3145732
  26.4 28.7 %all-to-all-start = ((bf16[4,128,1024]{2,1,0:T(8,128)(2,1)}), bf16[4,128,1024]{2,1,0:T(8,128)(2,1)S(1)}, u32[]{:S(2)}, u32[]{:S(2)}) async-start(bf16[4,128,1024]{2,1,0:T(8,128)(2,1)} %broadcast_in_dim.126), calls=%async_computation | async-start | bytes 2097152 | tf_op jit(solution)/shard_map/all_to_all | solution.py:71
  31.4 1.3 copy-start.7
  55.1 56.0 %all-to-all-start.1 = ((bf16[8,2,128,4,128]{2,4,3,1,0:T(8,128)(2,1)}), bf16[8,2,128,4,128]{2,4,3,1,0:T(8,128)(2,1)}, u32[]{:S(2)}, u32[]{:S(2)}) async-start(bf16[8,2,128,4,128]{2,4,3,1,0:T(8,128)(2,1)} %copy.25), calls=%async_computation.1 | async-start | bytes 4194304 | tf_op jit(solution)/shard_map/all_to_all | solution.py:60
  59.5 98.2 %all-reduce.2.cloned.1.call-start = ((), (), s32[]{:S(2)}) async-start(), calls=%async_computation.5 | async-start | bytes 4194304 | tf_op jit(solution)/shard_map/psum | solution.py:116
  63.2 0.7 copy-start.8
  63.8 4.6 %collective-permute-start.4 = (f32[3,4,128]{2,1,0:T(4,128)S(1)}, f32[3,4,128]{2,1,0:T(4,128)S(1)}, u32[]{:S(2)}, u32[]{:S(2)}) collective-permute-start(f32[3,4,128]{2,1,0:T(4,128)S(1)} %get-tuple-element.38), channel_id=1, source_target_pairs={{0,16},{8,24},{16,0},{24,8},{1,17},{9,25},{17,1},{25,9},{2,18},{10... | collective-permute-start | bytes 18440 | tf_op jit(solution)/shard_map/ppermute | solution.py:28
  66.3 3.6 %collective-permute-start.5 = (f32[3,4,128]{2,1,0:T(4,128)S(1)}, f32[3,4,128]{2,1,0:T(4,128)S(1)}, u32[]{:S(2)}, u32[]{:S(2)}) collective-permute-start(f32[3,4,128]{2,1,0:T(4,128)S(1)} %get-tuple-element.38), channel_id=1, source_target_pairs={{0,24},{8,0},{16,8},{24,16},{1,25},{9,1},{17,9},{25,17},{2,26},{10... | collective-permute-start | bytes 18440 | tf_op jit(solution)/shard_map/ppermute | solution.py:28
  67.7 5.4 %collective-permute-start.3 = (f32[3,4,128]{2,1,0:T(4,128)S(1)}, f32[3,4,128]{2,1,0:T(4,128)S(1)}, u32[]{:S(2)}, u32[]{:S(2)}) collective-permute-start(f32[3,4,128]{2,1,0:T(4,128)S(1)} %get-tuple-element.38), channel_id=1, source_target_pairs={{0,8},{8,16},{16,24},{24,0},{1,9},{9,17},{17,25},{25,1},{2,10},{10... | collective-permute-start | bytes 18440 | tf_op jit(solution)/shard_map/ppermute | solution.py:28
  75.5 2.2 %copy-start.1 = (bf16[4,128,1024]{2,1,0:T(8,128)(2,1)}, bf16[4,128,1024]{2,1,0:T(8,128)(2,1)S(1)}, u32[]{:S(2)}) copy-start(bf16[4,128,1024]{2,1,0:T(8,128)(2,1)S(1)} %multiply_convert_fusion.1) | copy-start | bytes 3145732
  84.9 11.3 %collective-permute-start.6 = (bf16[128,1024]{1,0:T(8,128)(2,1)}, bf16[128,1024]{1,0:T(8,128)(2,1)S(1)}, u32[]{:S(2)}, u32[]{:S(2)}) collective-permute-start(bf16[128,1024]{1,0:T(8,128)(2,1)} %get-tuple-element.36), channel_id=1, source_target_pairs={{0,8},{8,16},{16,24},{24,0},{1,9},{9,17},{17,25},{25,1},{2,10},{10... | collective-permute-start | bytes 786440 | tf_op jit(solution)/shard_map/ppermute | solution.py:39
  84.9 20.2 %collective-permute-start.7 = (bf16[128,1024]{1,0:T(8,128)(2,1)}, bf16[128,1024]{1,0:T(8,128)(2,1)S(1)}, u32[]{:S(2)}, u32[]{:S(2)}) collective-permute-start(bf16[128,1024]{1,0:T(8,128)(2,1)} %get-tuple-element.35), channel_id=1, source_target_pairs={{0,16},{8,24},{16,0},{24,8},{1,17},{9,25},{17,1},{25,9},{2,18},{10... | collective-permute-start | bytes 786440 | tf_op jit(solution)/shard_map/ppermute | solution.py:39
  85.4 19.6 %collective-permute-start.8 = (bf16[128,1024]{1,0:T(8,128)(2,1)}, bf16[128,1024]{1,0:T(8,128)(2,1)S(1)}, u32[]{:S(2)}, u32[]{:S(2)}) collective-permute-start(bf16[128,1024]{1,0:T(8,128)(2,1)} %get-tuple-element.34), channel_id=1, source_target_pairs={{0,24},{8,0},{16,8},{24,16},{1,25},{9,1},{17,9},{25,17},{2,26},{10... | collective-permute-start | bytes 786440 | tf_op jit(solution)/shard_map/ppermute | solution.py:39
  106.2 4.5 %copy-start.4 = (f32[128,1024]{1,0:T(8,128)S(1)}, f32[128,1024]{1,0:T(8,128)}, u32[]{:S(2)}) copy-start(f32[128,1024]{1,0:T(8,128)} %copy-done.3) | copy-start | bytes 1572868
  112.7 50.5 %all-to-all-start.2 = ((bf16[8,128,1024]{2,1,0:T(8,128)(2,1)}), bf16[8,128,1024]{2,1,0:T(8,128)(2,1)}, u32[]{:S(2)}, u32[]{:S(2)}) async-start(bf16[8,128,1024]{2,1,0:T(8,128)(2,1)} %broadcast_in_dim.134), calls=%async_computation.2 | async-start | bytes 4194304 | tf_op jit(solution)/shard_map/all_to_all | solution.py:132
  117.1 79.1 %reduce-scatter.2.cloned.1.call-start = ((), (), s32[]{:S(2)}) async-start(), calls=%async_computation.6 | async-start | bytes 1310720 | tf_op jit(solution)/shard_map/reduce_scatter | solution.py:145
  157.7 4.0 %copy-start = (f32[1024,1024]{1,0:T(8,128)S(1)}, f32[1024,1024]{1,0:T(8,128)}, u32[]{:S(2)}) copy-start(f32[1024,1024]{1,0:T(8,128)} %all-gather.2.cloned.1.call-done) | copy-start | bytes 12582916
  157.7 4.7 %copy-start.2 = (bf16[1024,1024]{1,0:T(8,128)(2,1)S(1)}, bf16[1024,1024]{1,0:T(8,128)(2,1)}, u32[]{:S(2)}) copy-start(bf16[1024,1024]{1,0:T(8,128)(2,1)} %all-reduce.2.cloned.1.call-done) | copy-start | bytes 6291460
Sparse Core Ops, SparseCore 0:
  13.2 39.2 all-gather.1
  88.8 68.7 all-reduce.1
  169.5 26.6 reduce-scatter.1
where the time goes:
time: 205 us
  waiting for transfers between devices  86.3 us (42%)
  matrix products  43.5 us (21%)
  starting transfers between devices  27.8 us (14%)
  other arithmetic  17.9 us (9%)
  local copies, waits for them, and re-layouts  15 us (7%)
  between operations  14 us (7%)
    psum x1, waiting for transfers between devices, body(): code_delta = lax.psum(code_sum, 'member').astype(jnp.float32)  37.8 us
    ppermute x3, waiting for transfers between devices, exchange(): lax.ppermute(sent, axis, [(i, (i + s) % size) for i in range(size)])  16.4 us
    all_gather x1, waiting for transfers between devices, body(): lax.all_gather(jnp.dot(code_feat, projection, preferred_element_type=jnp....  15 us
    reduce_scatter x1, waiting for transfers between devices, body(): lax.psum_scatter(sent_proj, 'group', scatter_dimension=0, tiled=True)  12.3 us
    ppermute x6, starting transfers between devices, shift_all(): lax.ppermute(x, axis, [(i, (i + s) % size) for i in range(size)])  11.5 us
    dot_general x1, matrix products, body(): jnp.einsum('qe,de->qd', dz_query, projection, preferred_element_type=jnp....  7.24 us
    dot_general x1, matrix products, body(): jnp.einsum('qe,de->qd', dz_code, projection, preferred_element_type=jnp.f...  7.24 us
    dot_general x1, matrix products, body(): jnp.dot(code_feat, projection, preferred_element_type=jnp.float32)  5.85 us
  transfers between devices with their start and end apart: 15, of which 8 were waited for; matrix products, arithmetic and copies ran while one was open for 30% of the time, Pallas kernels for 0%

commit v1 on v0

--- a/solution.py
+++ b/solution.py
@@ -6,6 +6,33 @@
 CB = 64
 inverse_temp = 120.0
 epsilon = 1e-06
+
+
+def case_set(point, dim_i):
+    point = jnp.moveaxis(point, 0, dim_i)
+    even = point.shape
+    return point.reshape(*even[:dim_i], even[dim_i] * even[dim_i + 1], *even[dim_i + 2 :])
+
+
+def balance_runs(payload, lane_axis, axis_k):
+    nodes = lax.psum(1, lane_axis)
+    stack_in = [(at, (at + 1) % nodes) for at in range(nodes)]
+    rows = [(to_i, src_i) for src_i, to_i in stack_in]
+    n_now, r_now = ([], [])
+    ix = 0
+    while ix < nodes - 1:
+        if ix % 2 == 0:
+            local_now = lax.ppermute(n_now[-1] if n_now else payload, lane_axis, stack_in)
+            n_now.append(local_now)
+        else:
+            r_now.append(lax.ppermute(r_now[-1] if r_now else payload, lane_axis, rows))
+        ix += 1
+    high = jnp.stack([*n_now[::-1], payload, *r_now])
+    ready = lax.axis_index(lane_axis)
+    last = len(n_now)
+    e_next = ready - last
+    high = high[(jnp.arange(nodes) - e_next) % nodes]
+    return case_set(high, axis_k)
 
 
 def embed(features, projection):
@@ -59,11 +86,8 @@
     feats = jnp.transpose(feats, (3, 0, 1, 2, 4))
     feat_cols = lax.all_to_all(feats, "member", split_axis=0, concat_axis=0, tiled=True)
     q_unit, q_inv, q_emb = embed(query_feat, projection)
-    code_values = lax.all_gather(
-        jnp.dot(code_feat, projection, preferred_element_type=jnp.float32),
-        "member",
-        axis=0,
-        tiled=True,
+    code_values = balance_runs(
+        jnp.dot(code_feat, projection, preferred_element_type=jnp.float32), "member", 0
     )
     c_inv = lax.rsqrt(jnp.sum(code_values * code_values, axis=1) + epsilon)
     c_unit = code_values * c_inv[:, None]

time: 205 us -> 243 us (1.19)
  local copies, waits for them, and re-layouts: 15 us -> 32.4 us
  starting transfers between devices: 27.8 us -> 37.3 us
  other arithmetic: 17.9 us -> 23 us
  waiting for transfers between devices: 86.3 us -> 90.8 us
    ppermute x0 -> x7, waiting for transfers between devices: none -> 20.4 us  [the longest x3 10.4 us: balance_runs(): r_now.append(lax.ppermute(r_now[-1] if r_now else payload, lane_axis, rows))]
    all_gather x1 -> x0, waiting for transfers between devices: 15 us -> none  [body(): lax.all_gather(jnp.dot(code_feat, projection, preferred_element_type=jnp....]
    unnamed x22 -> x31, local copies, waits for them, and re-layouts: 3.84 us -> 16.9 us
    ppermute x0 -> x7, starting transfers between devices: none -> 8.82 us  [the longest x3 8.26 us: balance_runs(): r_now.append(lax.ppermute(r_now[-1] if r_now else payload, lane_axis, rows))]
    gather x0 -> x1, local copies, waits for them, and re-layouts: none -> 4.95 us  [balance_runs(): high = high[(jnp.arange(nodes) - e_next) % nodes]]
    dot_general x4, matrix products: 4.6 us -> 8.56 us  [body(): term = jnp.dot(grad[g].T, q_all[g], preferred_element_type=jnp.float32)]
    dot_general x1, matrix products: 4.98 us -> 1.4 us  [embed(): values = jnp.dot(features, projection, preferred_element_type=jnp.float32)]
    ppermute x6, waiting for transfers between devices: 4.84 us -> 2.17 us  [shift_all(): lax.ppermute(x, axis, [(i, (i + s) % size) for i in range(size)])]
  transfers between devices with their start and end apart: 15 -> 21, of which waited for: 8 -> 9; matrix products, arithmetic and copies ran while one was open for 30% -> 34% of each run, Pallas kernels for 0% -> 0%
where the time goes in v1:
time: 243 us; the launch traced here: 242 us
  waiting for transfers between devices  90.8 us (37%)
  matrix products  44.3 us (18%)
  starting transfers between devices  37.3 us (15%)
  local copies, waits for them, and re-layouts  32.4 us (13%)
  other arithmetic  23 us (9%)
  between operations  14.4 us (6%)
    psum x1, waiting for transfers between devices, body(): code_delta = lax.psum(code_sum, 'member').astype(jnp.float32)  36.9 us
    unnamed x31, local copies, waits for them, and re-layouts  16.9 us
    ppermute x3, waiting for transfers between devices, exchange(): lax.ppermute(sent, axis, [(i, (i + s) % size) for i in range(size)])  16.8 us
    reduce_scatter x1, waiting for transfers between devices, body(): lax.psum_scatter(sent_proj, 'group', scatter_dimension=0, tiled=True)  14.5 us
    ppermute x6, starting transfers between devices, shift_all(): lax.ppermute(x, axis, [(i, (i + s) % size) for i in range(size)])  12.1 us
    ppermute x3, waiting for transfers between devices, balance_runs(): r_now.append(lax.ppermute(r_now[-1] if r_now else payload, lane_axis, rows))  10.4 us
    ppermute x4, waiting for transfers between devices, balance_runs(): lax.ppermute(n_now[-1] if n_now else payload, lane_axis, stack_in)  10 us
    dot_general x4, matrix products, body(): term = jnp.dot(grad[g].T, q_all[g], preferred_element_type=jnp.float32)  8.56 us
  transfers between devices with their start and end apart: 21, of which 9 were waited for; matrix products, arithmetic and copies ran while one was open for 34% of the time, Pallas kernels for 0%

profile of v1, /device:TPU:0, one launch (start us, length us, event | category | flops | bytes accessed | tf_op | source)
XLA Modules:
  0.0 242.1 jit_solution(17948256348385657618)
XLA Ops:
  7.2 5.9 %fusion.31 = f32[128,1024]{1,0:T(8,128)} fusion(bf16[128,4096]{1,0:T(8,128)(2,1)} %param.10, bf16[4096,1024]{1,0:T(8,128)(2,1)} %param.11), kind=kOutput, calls=%fused_computation.110 | convolution fusion | flops 1073741824 | bytes 9961472 | tf_op jit(solution)/shard_map/dot_general | solution.py:90
  13.6 2.9 %collective-permute-start.7 = (f32[128,1024]{1,0:T(8,128)}, f32[128,1024]{1,0:T(8,128)}, u32[]{:S(2)}, u32[]{:S(2)}) collective-permute-start(f32[128,1024]{1,0:T(8,128)} %fusion.31), channel_id=1, source_target_pairs={{1,0},{2,1},{3,2},{4,3},{5,4},{6,5},{7,6},{0,7},{9,8},{10,9},{11,1... | collective-permute-start | bytes 1572872 | tf_op jit(solution)/shard_map/ppermute | solution.py:28
  16.5 2.3 collective-permute-start
  18.8 2.6 %collective-permute-start.1 = (s32[16]{0:T(128)S(1)}, s32[16]{0:T(128)S(1)}, u32[]{:S(2)}, u32[]{:S(2)}) collective-permute-start(s32[16]{0:T(128)S(1)} %bitcast.157), channel_id=1, source_target_pairs={{0,16},{8,24},{16,0},{24,8},{1,17},{9,25},{17,1},{25,9},{2,18},{10... | collective-permute-start | bytes 200 | tf_op jit(solution)/shard_map/ppermute | solution.py:55
  21.4 1.3 collective-permute-start.2
  22.7 1.4 multiply_reduce_fusion.2
  24.3 1.1 broadcast_in_dim.127
  25.4 4.3 %all-to-all-start = ((bf16[4,128,1024]{2,1,0:T(8,128)(2,1)}), bf16[4,128,1024]{2,1,0:T(8,128)(2,1)}, u32[]{:S(2)}, u32[]{:S(2)}) async-start(bf16[4,128,1024]{2,1,0:T(8,128)(2,1)} %broadcast_in_dim.127), calls=%async_computation | async-start | bytes 2097152 | tf_op jit(solution)/shard_map/all_to_all | solution.py:95
  29.8 9.5 %collective-permute-done.4 = f32[128,1024]{1,0:T(8,128)} collective-permute-done((f32[128,1024]{1,0:T(8,128)S(1)}, f32[128,1024]{1,0:T(8,128)}, u32[]{:S(2)}, u32[]{:S(2)}) %collective-permute-start.4) | collective-permute-done | bytes 524320 | tf_op jit(solution)/shard_map/ppermute | solution.py:25
  39.4 1.3 copy.23
  40.6 1.3 copy.24
  42.0 1.7 maximum_bitcast_fusion
  43.8 1.6 copy.25
  46.0 2.7 %collective-permute-start.8 = (f32[128,1024]{1,0:T(8,128)}, f32[128,1024]{1,0:T(8,128)S(1)}, u32[]{:S(2)}, u32[]{:S(2)}) collective-permute-start(f32[128,1024]{1,0:T(8,128)} %collective-permute-done.7), channel_id=1, source_target_pairs={{1,0},{2,1},{3,2},{4,3},{5,4},{6,5},{7,6},{0,7},{9,8},{10,9},{11,1... | collective-permute-start | bytes 1572872 | tf_op jit(solution)/shard_map/ppermute | solution.py:28
  49.6 10.4 %collective-permute-done.8 = f32[128,1024]{1,0:T(8,128)S(1)} collective-permute-done((f32[128,1024]{1,0:T(8,128)}, f32[128,1024]{1,0:T(8,128)S(1)}, u32[]{:S(2)}, u32[]{:S(2)}) %collective-permute-start.8) | collective-permute-done | bytes 524320 | tf_op jit(solution)/shard_map/ppermute | solution.py:28
  60.0 2.7 %collective-permute-start.9 = (f32[128,1024]{1,0:T(8,128)S(1)}, f32[128,1024]{1,0:T(8,128)S(1)}, u32[]{:S(2)}, u32[]{:S(2)}) collective-permute-start(f32[128,1024]{1,0:T(8,128)S(1)} %collective-permute-done.8), channel_id=1, source_target_pairs={{1,0},{2,1},{3,2},{4,3},{5,4},{6,5},{7,6},{0,7},{9,8},{10,9},{11,1... | collective-permute-start | bytes 1572872 | tf_op jit(solution)/shard_map/ppermute | solution.py:28
  62.7 0.9 bitcast_dynamic-update-slice_fusion.7
  63.6 1.9 bitcast_dynamic-update-slice_fusion.6
  65.5 1.9 bitcast_dynamic-update-slice_fusion.5
  67.4 1.9 bitcast_dynamic-update-slice_fusion.4
  69.3 1.9 bitcast_dynamic-update-slice_fusion.3
  71.2 1.9 bitcast_dynamic-update-slice_fusion.2
  73.1 0.8 bitcast_dynamic-update-slice_fusion.1
  73.9 0.9 bitcast_dynamic-update-slice_fusion
  74.8 4.9 %gather_fusion.1 = f32[8,128,1024]{2,1,0:T(8,128)} fusion(f32[8,128,1024]{2,1,0:T(8,128)} %bitcast_dynamic-update-slice_fusion, s32[1024]{0:T(1024)S(1)} %pad_clamp_fusion), kind=kCustom, calls=%fused_computation.1 | custom fusion | bytes 8388640 | tf_op jit(solution)/shard_map/gather | solution.py:34
  79.8 2.7 %multiply_reduce_fusion = f32[8,128]{1,0:T(8,128)S(1)} fusion(f32[8,128,1024]{2,1,0:T(8,128)} %gather_fusion.1), kind=kLoop, calls=%fused_computation.13 | loop fusion | flops 2096128 | bytes 4198400 | tf_op jit(solution)/shard_map/reduce_sum | solution.py:92
  82.5 0.8 copy-done.1
  83.2 1.6 fusion.3
  84.9 3.6 %all-to-all-start.1 = ((bf16[8,2,128,4,128]{2,4,3,1,0:T(8,128)(2,1)}), bf16[8,2,128,4,128]{2,4,3,1,0:T(8,128)(2,1)S(1)}, u32[]{:S(2)}, u32[]{:S(2)}) async-start(bf16[8,2,128,4,128]{2,4,3,1,0:T(8,128)(2,1)} %copy.25), calls=%async_computation.1 | async-start | bytes 4194304 | tf_op jit(solution)/shard_map/all_to_all | solution.py:87
  88.5 3.3 %fusion.29 = (f32[4,128]{1,0:T(4,128)S(1)}, f32[4,128,1024]{2,1,0:T(8,128)S(1)}) fusion(bf16[4,128,1024]{2,1,0:T(8,128)(2,1)} %all-to-all-done, bf16[1024,1024]{1,0:T(8,128)(2,1)} %fusion.3, pred[4,1024]{1,0:T(4,128)(4,1)S(1)} %broadcast_in_dim.125), kind=kOutput, calls=%fused_computation.108 | convolution fusion | flops 1075314176 | bytes 5249024 | tf_op jit(solution)/shard_map/gqe,ke->gqk/dot_general | solution.py:110
  91.8 1.3 copy-done.4
  93.7 2.0 collective-permute-start.10
  95.7 2.4 collective-permute-start.11
  98.1 1.5 collective-permute-start.12
  99.6 0.7 collective-permute-done.11
  100.3 1.5 collective-permute-done.12
  102.5 2.1 multiply_convert_fusion
  104.6 1.9 fusion.14
  106.5 1.7 fusion.15
  108.1 1.7 fusion.13
  109.8 3.3 %add_convert_fusion = bf16[1024,1024]{1,0:T(8,128)(2,1)} fusion(f32[1024,1024]{1,0:T(8,128)S(1)} %fusion.13, f32[1024,1024]{1,0:T(8,128)S(1)} %fusion.14, f32[1024,1024]{1,0:T(8,128)S(1)} %fusion.15, pred[]{:T(512)S(6)} %eq.77, pred[]{:T(512)S(6)} %eq.76, pred[]{:T(512)S(6)} %eq.75, pred[]{:T(512)S(6)} %eq.74, bf16[4,128,1024]{2,1,0:T(8,128)(2,1)} %all-to-all-done, ...), kind=kOutput, calls=%fused_computation.12 | convolution fusion | flops 285212672 | bytes 15204356 | tf_op jit(solution)/shard_map/dot_general | solution.py:135
  113.2 4.5 %fusion.30 = (bf16[4,128,1024]{2,1,0:T(8,128)(2,1)S(1)}, f32[4,128,1024]{2,1,0:T(8,128)}) fusion(bf16[4,128,1024]{2,1,0:T(8,128)(2,1)} %copy-done.7, bf16[1024,1024]{1,0:T(8,128)(2,1)} %fusion.3), kind=kOutput, calls=%fused_computation.109 | convolution fusion | flops 1074266112 | bytes 6291456 | tf_op jit(solution)/shard_map/gqk,ke->gqe/dot_general | solution.py:141
  117.7 0.8 dynamic-slice_select_fusion
  118.6 3.7 %collective-permute-start.14 = (bf16[128,1024]{1,0:T(8,128)(2,1)S(1)}, bf16[128,1024]{1,0:T(8,128)(2,1)}, u32[]{:S(2)}, u32[]{:S(2)}) collective-permute-start(bf16[128,1024]{1,0:T(8,128)(2,1)S(1)} %get-tuple-element.35), channel_id=1, source_target_pairs={{0,16},{8,24},{16,0},{24,8},{1,17},{9,25},{17,1},{25,9},{2,18},{10... | collective-permute-start | bytes 786440 | tf_op jit(solution)/shard_map/ppermute | solution.py:66
  122.3 7.5 %collective-permute-done.13 = bf16[128,1024]{1,0:T(8,128)(2,1)} collective-permute-done((bf16[128,1024]{1,0:T(8,128)(2,1)}, bf16[128,1024]{1,0:T(8,128)(2,1)}, u32[]{:S(2)}, u32[]{:S(2)}) %collective-permute-start.13) | collective-permute-done | bytes 262176 | tf_op jit(solution)/shard_map/ppermute | solution.py:66
  129.9 9.2 %collective-permute-done.14 = bf16[128,1024]{1,0:T(8,128)(2,1)} collective-permute-done((bf16[128,1024]{1,0:T(8,128)(2,1)S(1)}, bf16[128,1024]{1,0:T(8,128)(2,1)}, u32[]{:S(2)}, u32[]{:S(2)}) %collective-permute-start.14) | collective-permute-done | bytes 262176 | tf_op jit(solution)/shard_map/ppermute | solution.py:66
  139.1 2.2 pad_maximum_fusion
  141.3 2.8 %gather_fusion.3 = bf16[4,128,1024]{2,1,0:T(8,128)(2,1)} fusion(bf16[4,128,1024]{2,1,0:T(8,128)(2,1)} %pad_maximum_fusion, s32[1024]{0:T(1024)S(1)} %pad_clamp_fusion.1), kind=kCustom, calls=%fused_computation.3 | custom fusion | bytes 2097168 | tf_op jit(solution)/shard_map/jit(_take)/gather | solution.py:68
  144.1 1.6 select_reduce_fusion
  145.8 1.3 multiply_reduce_fusion.1
  147.1 1.2 multiply_convert_fusion.1
  148.3 1.6 broadcast_in_dim.135
  149.9 4.4 %all-to-all-start.2 = ((bf16[8,128,1024]{2,1,0:T(8,128)(2,1)}), bf16[8,128,1024]{2,1,0:T(8,128)(2,1)}, u32[]{:S(2)}, u32[]{:S(2)}) async-start(bf16[8,128,1024]{2,1,0:T(8,128)(2,1)} %broadcast_in_dim.135), calls=%async_computation.2 | async-start | bytes 4194304 | tf_op jit(solution)/shard_map/all_to_all | solution.py:156
  154.6 1.2 fusion.28
  155.7 36.9 %all-reduce.2.cloned.1.call-done = bf16[1024,1024]{1,0:T(8,128)(2,1)} async-done(((bf16[1024,1024]{1,0:T(8,128)(2,1)}), bf16[1024,1024]{1,0:T(8,128)(2,1)}) %all-reduce.2.cloned.1.call-update) | async-done | bytes 2097168 | tf_op jit(solution)/shard_map/psum | solution.py:140
  192.6 3.7 %fusion = f32[1024]{0:T(1024)S(1)} fusion(bf16[1024,1024]{1,0:T(8,128)(2,1)} %all-reduce.2.cloned.1.call-done, f32[8,128,1024]{2,1,0:T(8,128)} %gather_fusion.1, f32[1024]{0:T(1024)S(1)} %rsqrt_bitcast_fusion), kind=kLoop, calls=%fused_computation.8 | loop fusion | flops 4193280 | bytes 6299648 | tf_op jit(solution)/shard_map/reduce_sum | solution.py:46
  196.6 0.7 copy-done.3
  197.3 0.8 fusion.2
  198.1 3.2 %fusion.4 = f32[4,128,1024,1]{2,1,3,0:T(8,128)S(1)} fusion(bf16[8,128,1024]{2,1,0:T(8,128)(2,1)} %all-to-all-done.2, bf16[8,1,128,4,128]{2,4,3,1,0:T(8,128)(2,1)} %get-tuple-element.32), kind=kOutput, calls=%fused_computation.17 | convolution fusion | flops 1073741824 | bytes 5242880 | tf_op jit(solution)/shard_map/mqgr,mqe->gre/dot_general | solution.py:164
  201.3 2.9 %select_convert_fusion = (bf16[4,128,1024]{2,1,0:T(8,128)(2,1)}, f32[4,128,1024]{2,1,0:T(8,128)}) fusion(pred[4]{0:T(512)(128)(4,1)S(1)} %iota_compare_fusion.1, bf16[8,128,1024,1]{2,1,0,3:T(8,128)(2,1)S(1)} %bitcast.147, bf16[8,1,128,4,128]{2,4,3,1,0:T(8,128)(2,1)S(1)} %get-tuple-element.31, f32[4,128,1024,1]{2,1,3,0:T(8,128)S(1)} %fusion.4), kind=kOutput, calls=%fused_computation.23 | convolution fusion | flops 1074790400 | bytes 8388612 | tf_op jit(solution)/shard_map/mqgr,mqe->gre/dot_general | solution.py:166
  204.3 7.2 %convolution_convert_fusion.1 = bf16[128,4096]{1,0:T(8,128)(2,1)} fusion(bf16[128,1024]{1,0:T(8,128)(2,1)S(1)} %multiply_convert_fusion.1, bf16[4096,1024]{1,0:T(8,128)(2,1)} %param.11), kind=kOutput, calls=%fused_computation.7 | convolution fusion | flops 1074266112 | bytes 9699328 | tf_op jit(solution)/shard_map/qe,de->qd/dot_general | solution.py:150
  211.5 7.3 %convolution_convert_fusion = bf16[128,4096]{1,0:T(8,128)(2,1)} fusion(bf16[4096,1024]{1,0:T(8,128)(2,1)} %param.11, bf16[1024,1024]{1,0:T(8,128)(2,1)S(1)} %fusion.2, s32[]{:T(128)S(6)} %select_n.178), kind=kOutput, calls=%fused_computation.6 | convolution fusion | flops 1074266112 | bytes 9699332 | tf_op jit(solution)/shard_map/qe,de->qd/dot_general | solution.py:153
  218.8 14.5 %reduce-scatter.2.cloned.1.call-done = bf16[1,128,1024]{2,1,0:T(8,128)(2,1)} async-done(((bf16[4,128,1024]{2,1,0:T(8,128)(2,1)}), bf16[1,128,1024]{2,1,0:T(8,128)(2,1)}) %reduce-scatter.2.cloned.1.call-update) | async-done | bytes 262160 | tf_op jit(solution)/shard_map/reduce_scatter | solution.py:169
  233.3 2.0 convert_add_fusion
  (73 shorter events, 4.4 us)
Async XLA Ops:
  7.2 15.6 %copy-start = (bf16[4096,1024]{1,0:T(8,128)(2,1)S(1)}, bf16[4096,1024]{1,0:T(8,128)(2,1)}, u32[]{:S(2)}) copy-start(bf16[4096,1024]{1,0:T(8,128)(2,1)} %param.11) | copy-start | bytes 25165828
  7.2 9.3 %copy-start.10 = (s32[1,16]{1,0:T(1,128)S(1)}, s32[1,16]{1,0:T(1,128)}, u32[]{:S(2)}) copy-start(s32[1,16]{1,0:T(1,128)} %param.12) | copy-start | bytes 196
  7.2 15.6 %copy-start.5 = (bf16[128,4096]{1,0:T(8,128)(2,1)S(1)}, bf16[128,4096]{1,0:T(8,128)(2,1)}, u32[]{:S(2)}) copy-start(bf16[128,4096]{1,0:T(8,128)(2,1)} %param.9) | copy-start | bytes 3145732
  13.1 16.6 %collective-permute-start.3 = (f32[128,1024]{1,0:T(8,128)}, f32[128,1024]{1,0:T(8,128)S(1)}, u32[]{:S(2)}, u32[]{:S(2)}) collective-permute-start(f32[128,1024]{1,0:T(8,128)} %fusion.31), channel_id=1, source_target_pairs={{0,1},{1,2},{2,3},{3,4},{4,5},{5,6},{6,7},{7,0},{8,9},{9,10},{10,1... | collective-permute-start | bytes 1572872 | tf_op jit(solution)/shard_map/ppermute | solution.py:25
  13.6 32.4 %collective-permute-start.7 = (f32[128,1024]{1,0:T(8,128)}, f32[128,1024]{1,0:T(8,128)}, u32[]{:S(2)}, u32[]{:S(2)}) collective-permute-start(f32[128,1024]{1,0:T(8,128)} %fusion.31), channel_id=1, source_target_pairs={{1,0},{2,1},{3,2},{4,3},{5,4},{6,5},{7,6},{0,7},{9,8},{10,9},{11,1... | collective-permute-start | bytes 1572872 | tf_op jit(solution)/shard_map/ppermute | solution.py:28
  16.5 28.9 %collective-permute-start = (s32[16]{0:T(128)S(1)}, s32[16]{0:T(128)S(1)}, u32[]{:S(2)}, u32[]{:S(2)}) collective-permute-start(s32[16]{0:T(128)S(1)} %bitcast.156), channel_id=1, source_target_pairs={{0,8},{8,16},{16,24},{24,0},{1,9},{9,17},{17,25},{25,1},{2,10},{10... | collective-permute-start | bytes 200 | tf_op jit(solution)/shard_map/ppermute | solution.py:55
  18.8 26.6 %collective-permute-start.1 = (s32[16]{0:T(128)S(1)}, s32[16]{0:T(128)S(1)}, u32[]{:S(2)}, u32[]{:S(2)}) collective-permute-start(s32[16]{0:T(128)S(1)} %bitcast.157), channel_id=1, source_target_pairs={{0,16},{8,24},{16,0},{24,8},{1,17},{9,25},{17,1},{25,9},{2,18},{10... | collective-permute-start | bytes 200 | tf_op jit(solution)/shard_map/ppermute | solution.py:55
  21.4 24.0 %collective-permute-start.2 = (s32[16]{0:T(128)S(1)}, s32[16]{0:T(128)S(1)}, u32[]{:S(2)}, u32[]{:S(2)}) collective-permute-start(s32[16]{0:T(128)S(1)} %bitcast.158), channel_id=1, source_target_pairs={{0,24},{8,0},{16,8},{24,16},{1,25},{9,1},{17,9},{25,17},{2,26},{10... | collective-permute-start | bytes 200 | tf_op jit(solution)/shard_map/ppermute | solution.py:55
  24.1 16.5 %copy-start.6 = (bf16[128,4096]{1,0:T(8,128)(2,1)S(1)}, bf16[128,4096]{1,0:T(8,128)(2,1)}, u32[]{:S(2)}) copy-start(bf16[128,4096]{1,0:T(8,128)(2,1)} %param.10) | copy-start | bytes 3145732
  25.4 59.5 %all-to-all-start = ((bf16[4,128,1024]{2,1,0:T(8,128)(2,1)}), bf16[4,128,1024]{2,1,0:T(8,128)(2,1)}, u32[]{:S(2)}, u32[]{:S(2)}) async-start(bf16[4,128,1024]{2,1,0:T(8,128)(2,1)} %broadcast_in_dim.127), calls=%async_computation | async-start | bytes 2097152 | tf_op jit(solution)/shard_map/all_to_all | solution.py:95
  29.7 12.3 %copy-start.8 = (f32[128,1024]{1,0:T(8,128)}, f32[128,1024]{1,0:T(8,128)S(1)}, u32[]{:S(2)}) copy-start(f32[128,1024]{1,0:T(8,128)S(1)} %collective-permute-done.3) | copy-start | bytes 1572868
  29.7 9.7 %collective-permute-start.4 = (f32[128,1024]{1,0:T(8,128)S(1)}, f32[128,1024]{1,0:T(8,128)}, u32[]{:S(2)}, u32[]{:S(2)}) collective-permute-start(f32[128,1024]{1,0:T(8,128)S(1)} %collective-permute-done.3), channel_id=1, source_target_pairs={{0,1},{1,2},{2,3},{3,4},{4,5},{5,6},{6,7},{7,0},{8,9},{9,10},{10,1... | collective-permute-start | bytes 1572872 | tf_op jit(solution)/shard_map/ppermute | solution.py:25
  39.3 9.8 %collective-permute-start.5 = (f32[128,1024]{1,0:T(8,128)}, f32[128,1024]{1,0:T(8,128)}, u32[]{:S(2)}, u32[]{:S(2)}) collective-permute-start(f32[128,1024]{1,0:T(8,128)} %collective-permute-done.4), channel_id=1, source_target_pairs={{0,1},{1,2},{2,3},{3,4},{4,5},{5,6},{6,7},{7,0},{8,9},{9,10},{10,1... | collective-permute-start | bytes 1572872 | tf_op jit(solution)/shard_map/ppermute | solution.py:25
  46.0 14.0 %collective-permute-start.8 = (f32[128,1024]{1,0:T(8,128)}, f32[128,1024]{1,0:T(8,128)S(1)}, u32[]{:S(2)}, u32[]{:S(2)}) collective-permute-start(f32[128,1024]{1,0:T(8,128)} %collective-permute-done.7), channel_id=1, source_target_pairs={{1,0},{2,1},{3,2},{4,3},{5,4},{6,5},{7,6},{0,7},{9,8},{10,9},{11,1... | collective-permute-start | bytes 1572872 | tf_op jit(solution)/shard_map/ppermute | solution.py:28
  49.2 13.6 %collective-permute-start.6 = (f32[128,1024]{1,0:T(8,128)}, f32[128,1024]{1,0:T(8,128)S(1)}, u32[]{:S(2)}, u32[]{:S(2)}) collective-permute-start(f32[128,1024]{1,0:T(8,128)} %collective-permute-done.5), channel_id=1, source_target_pairs={{0,1},{1,2},{2,3},{3,4},{4,5},{5,6},{6,7},{7,0},{8,9},{9,10},{10,1... | collective-permute-start | bytes 1572872 | tf_op jit(solution)/shard_map/ppermute | solution.py:25
  60.0 13.9 %collective-permute-start.9 = (f32[128,1024]{1,0:T(8,128)S(1)}, f32[128,1024]{1,0:T(8,128)S(1)}, u32[]{:S(2)}, u32[]{:S(2)}) collective-permute-start(f32[128,1024]{1,0:T(8,128)S(1)} %collective-permute-done.8), channel_id=1, source_target_pairs={{1,0},{2,1},{3,2},{4,3},{5,4},{6,5},{7,6},{0,7},{9,8},{10,9},{11,1... | collective-permute-start | bytes 1572872 | tf_op jit(solution)/shard_map/ppermute | solution.py:28
  79.8 3.4 %copy-start.1 = (f32[8,128,1024]{2,1,0:T(8,128)S(1)}, f32[8,128,1024]{2,1,0:T(8,128)}, u32[]{:S(2)}) copy-start(f32[8,128,1024]{2,1,0:T(8,128)} %gather_fusion.1) | copy-start | bytes 12582916
  84.9 63.4 %all-to-all-start.1 = ((bf16[8,2,128,4,128]{2,4,3,1,0:T(8,128)(2,1)}), bf16[8,2,128,4,128]{2,4,3,1,0:T(8,128)(2,1)S(1)}, u32[]{:S(2)}, u32[]{:S(2)}) async-start(bf16[8,2,128,4,128]{2,4,3,1,0:T(8,128)(2,1)} %copy.25), calls=%async_computation.1 | async-start | bytes 4194304 | tf_op jit(solution)/shard_map/all_to_all | solution.py:87
  88.5 5.2 %copy-start.9 = (f32[128]{0:T(128)S(1)}, f32[128]{0:T(128)}, u32[]{:S(2)}) copy-start(f32[128]{0:T(128)} %param.13) | copy-start | bytes 1540
  88.5 104.1 %all-reduce.2.cloned.1.call-start = ((), (), s32[]{:S(2)}) async-start(), calls=%async_computation.4 | async-start | bytes 4194304 | tf_op jit(solution)/shard_map/psum | solution.py:140
  91.8 1.3 copy-start.4
  93.7 5.9 %collective-permute-start.10 = (f32[3,4,128]{2,1,0:T(4,128)S(1)}, f32[3,4,128]{2,1,0:T(4,128)S(1)}, u32[]{:S(2)}, u32[]{:S(2)}) collective-permute-start(f32[3,4,128]{2,1,0:T(4,128)S(1)} %get-tuple-element.38), channel_id=1, source_target_pairs={{0,8},{8,16},{16,24},{24,0},{1,9},{9,17},{17,25},{25,1},{2,10},{10... | collective-permute-start | bytes 18440 | tf_op jit(solution)/shard_map/ppermute | solution.py:55
  95.7 4.5 %collective-permute-start.11 = (f32[3,4,128]{2,1,0:T(4,128)S(1)}, f32[3,4,128]{2,1,0:T(4,128)S(1)}, u32[]{:S(2)}, u32[]{:S(2)}) collective-permute-start(f32[3,4,128]{2,1,0:T(4,128)S(1)} %get-tuple-element.38), channel_id=1, source_target_pairs={{0,16},{8,24},{16,0},{24,8},{1,17},{9,25},{17,1},{25,9},{2,18},{10... | collective-permute-start | bytes 18440 | tf_op jit(solution)/shard_map/ppermute | solution.py:55
  98.1 3.6 %collective-permute-start.12 = (f32[3,4,128]{2,1,0:T(4,128)S(1)}, f32[3,4,128]{2,1,0:T(4,128)S(1)}, u32[]{:S(2)}, u32[]{:S(2)}) collective-permute-start(f32[3,4,128]{2,1,0:T(4,128)S(1)} %get-tuple-element.38), channel_id=1, source_target_pairs={{0,24},{8,0},{16,8},{24,16},{1,25},{9,1},{17,9},{25,17},{2,26},{10... | collective-permute-start | bytes 18440 | tf_op jit(solution)/shard_map/ppermute | solution.py:55
  104.6 5.2 %copy-start.7 = (bf16[4,128,1024]{2,1,0:T(8,128)(2,1)}, bf16[4,128,1024]{2,1,0:T(8,128)(2,1)S(1)}, u32[]{:S(2)}) copy-start(bf16[4,128,1024]{2,1,0:T(8,128)(2,1)S(1)} %multiply_convert_fusion) | copy-start | bytes 3145732
  118.5 11.4 %collective-permute-start.13 = (bf16[128,1024]{1,0:T(8,128)(2,1)}, bf16[128,1024]{1,0:T(8,128)(2,1)}, u32[]{:S(2)}, u32[]{:S(2)}) collective-permute-start(bf16[128,1024]{1,0:T(8,128)(2,1)} %get-tuple-element.36), channel_id=1, source_target_pairs={{0,8},{8,16},{16,24},{24,0},{1,9},{9,17},{17,25},{25,1},{2,10},{10... | collective-permute-start | bytes 786440 | tf_op jit(solution)/shard_map/ppermute | solution.py:66
  118.6 20.5 %collective-permute-start.14 = (bf16[128,1024]{1,0:T(8,128)(2,1)S(1)}, bf16[128,1024]{1,0:T(8,128)(2,1)}, u32[]{:S(2)}, u32[]{:S(2)}) collective-permute-start(bf16[128,1024]{1,0:T(8,128)(2,1)S(1)} %get-tuple-element.35), channel_id=1, source_target_pairs={{0,16},{8,24},{16,0},{24,8},{1,17},{9,25},{17,1},{25,9},{2,18},{10... | collective-permute-start | bytes 786440 | tf_op jit(solution)/shard_map/ppermute | solution.py:66
  122.3 16.8 %collective-permute-start.15 = (bf16[128,1024]{1,0:T(8,128)(2,1)S(1)}, bf16[128,1024]{1,0:T(8,128)(2,1)}, u32[]{:S(2)}, u32[]{:S(2)}) collective-permute-start(bf16[128,1024]{1,0:T(8,128)(2,1)S(1)} %get-tuple-element.34), channel_id=1, source_target_pairs={{0,24},{8,0},{16,8},{24,16},{1,25},{9,1},{17,9},{25,17},{2,26},{10... | collective-permute-start | bytes 786440 | tf_op jit(solution)/shard_map/ppermute | solution.py:66
  149.9 48.3 %all-to-all-start.2 = ((bf16[8,128,1024]{2,1,0:T(8,128)(2,1)}), bf16[8,128,1024]{2,1,0:T(8,128)(2,1)}, u32[]{:S(2)}, u32[]{:S(2)}) async-start(bf16[8,128,1024]{2,1,0:T(8,128)(2,1)} %broadcast_in_dim.135), calls=%async_computation.2 | async-start | bytes 4194304 | tf_op jit(solution)/shard_map/all_to_all | solution.py:156
  154.3 79.0 %reduce-scatter.2.cloned.1.call-start = ((), (), s32[]{:S(2)}) async-start(), calls=%async_computation.5 | async-start | bytes 1310720 | tf_op jit(solution)/shard_map/reduce_scatter | solution.py:169
  192.6 4.0 %copy-start.2 = (f32[8,128,1024]{2,1,0:T(8,128)S(1)}, f32[8,128,1024]{2,1,0:T(8,128)}, u32[]{:S(2)}) copy-start(f32[8,128,1024]{2,1,0:T(8,128)} %gather_fusion.1) | copy-start | bytes 12582916
  192.6 4.7 %copy-start.3 = (bf16[1024,1024]{1,0:T(8,128)(2,1)S(1)}, bf16[1024,1024]{1,0:T(8,128)(2,1)}, u32[]{:S(2)}) copy-start(bf16[1024,1024]{1,0:T(8,128)(2,1)} %all-reduce.2.cloned.1.call-done) | copy-start | bytes 6291460
Sparse Core Ops, SparseCore 0:
  122.4 70.1 all-reduce.1
  204.4 28.8 reduce-scatter.1
